TPU v7x, 32 devices: a whole 2x2x4 slice. The times are simulated.
32 devices in a mesh: ep: 16 (over z, x, core), dp: 2 (over y).
Axes of the slice: x: 2, y: 2, z: 4, core: 2. Of those that a mesh axis runs over, the one named last changes fastest.
Arguments:
- tokens: bfloat16 [1024, 4096], P('ep', 'dp'), may hold values from -6 to 6
- expert_ids: int32 [1024, 8], P('ep'), may hold values from 0 to 15, all different within a row
- gate_logits: float32 [1024, 8], P('ep'), may hold values from -6 to 6
- placement: int32 [8], replicated, may hold values from 0 to 15, as said below
- split_rows: int32 [8], replicated, may hold values from 0 to 32
- gate_up_weight: bfloat16 [16, 4096, 2, 1024], P('ep', None, None, 'dp'), may hold values from -0.09375 to 0.09375
- down_weight: bfloat16 [16, 1024, 4096], P('ep', None, 'dp'), may hold values from -0.1875 to 0.1875
- spare_gate_up: bfloat16 [16, 4096, 2, 512], P('ep', None, None, 'dp'), may hold values from -0.09375 to 0.09375
- spare_down: bfloat16 [16, 512, 4096], P('ep', None, 'dp'), may hold values from -0.1875 to 0.1875
Outputs:
- mixed: bfloat16 [1024, 4096], P('ep', 'dp')
Inputs may be any that keep to these rules, and one draw needn't show every extreme that they name: `expert_ids`: each token names 8 different experts. `placement`: 8 different experts.
All inputs are finite; a program needn't handle non-finite values.
Results may differ from a plain program's by a relative error of at most 0.0058.
Values may be sent and summed in bfloat16 or wider, within the bound.
No kernel may reach another device: no remote copies, remote signals or barrier semaphores. Data moves between devices by JAX's collectives and lax.ppermute only.
A program may use at most 64 MiB of HBM per device.

v0:
```python
import jax
import jax.numpy as jnp
from jax import lax
from jax.sharding import PartitionSpec as P


def gate_up(row_block, weight):
    gate_both = jnp.einsum("rd,djf->rjf", row_block, weight, preferred_element_type=jnp.float32)
    return (jax.nn.silu(gate_both[:, 0, :]) * gate_both[:, 1, :]).astype(jnp.bfloat16)


def slot_tables(ids, target, low, limit, capacity, top_count):
    groups, per_group = ids.shape
    hit = ids == target
    ordinal = jnp.arange(per_group, dtype=jnp.int32)
    earlier = (ordinal[None, :] < ordinal[:, None]).astype(jnp.bfloat16)
    rank = jnp.einsum(
        "pq,gq->gp", earlier, hit.astype(jnp.bfloat16), preferred_element_type=jnp.float32
    ).astype(jnp.int32)
    position = rank - low
    kept = hit & (position >= 0) & (position < limit)
    group_tokens = per_group // top_count
    token = (
        jnp.arange(groups, dtype=jnp.int32)[:, None] * group_tokens + ordinal[None, :] // top_count
    )
    slots = jnp.arange(capacity, dtype=jnp.int32)
    sel = kept[:, :, None] & (position[:, :, None] == slots[None, None, :])
    row_of_slot = jnp.sum(jnp.where(sel, token[:, :, None], 0), axis=1)
    flat = jnp.arange(groups, dtype=jnp.int32)[:, None] * capacity + position
    return (row_of_slot.reshape(-1), kept, flat)


def per_token(kept, flat, weight, group_tokens, top_count):
    groups = kept.shape[0]
    kept = kept.reshape(groups * group_tokens, top_count)
    flat = flat.reshape(groups * group_tokens, top_count)
    index = jnp.sum(jnp.where(kept, flat, 0), axis=1)
    scale = jnp.sum(jnp.where(kept, weight, 0.0), axis=1)
    return (index, scale)


def per_device(
    tokens,
    expert_ids,
    gate_logits,
    placement,
    split_rows,
    gate_up_weight,
    down_weight,
    spare_gate_up,
    spare_down,
):
    ep_count = lax.axis_size("ep")
    me = lax.axis_index("ep")
    group_tokens = tokens.shape[0]
    top_count = expert_ids.shape[1]
    spares = placement.shape[0]
    halves = spare_gate_up.shape[0] * ep_count // spares
    capacity = group_tokens * top_count // ep_count
    per_group = group_tokens * top_count
    whole_rows = lax.all_gather(tokens, "dp", axis=1, tiled=True)
    every_row = lax.all_gather(whole_rows, "ep", axis=0, tiled=True)
    every_id = lax.all_gather(expert_ids, "ep", axis=0, tiled=True)
    every_logit = lax.all_gather(gate_logits, "ep", axis=0, tiled=True)
    ids = every_id.reshape(ep_count, per_group)
    gate_score = jax.nn.sigmoid(every_logit)
    gate_weight = 2.5 * gate_score / jnp.sum(gate_score, axis=1, keepdims=True)
    is_match = placement == me
    home_limit = jnp.where(
        jnp.any(is_match),
        jnp.minimum(jnp.sum(jnp.where(is_match, split_rows, 0)), capacity),
        capacity,
    )
    home_rows_of, home_kept, home_flat = slot_tables(ids, me, 0, home_limit, capacity, top_count)
    spare_index = me // halves
    spare_rows_of, spare_kept, spare_flat = slot_tables(
        ids, placement[spare_index], split_rows[spare_index], capacity, capacity, top_count
    )
    home_rows = jnp.take(every_row, home_rows_of, axis=0)
    spare_rows = jnp.take(every_row, spare_rows_of, axis=0)
    home_hidden = gate_up(home_rows, gate_up_weight[0])
    spare_hidden = gate_up(spare_rows, spare_gate_up[0])
    home_hidden = lax.all_gather(home_hidden, "dp", axis=1, tiled=True)
    spare_hidden = lax.all_gather(spare_hidden, "dp", axis=1, tiled=True)
    home_out = jnp.dot(home_hidden, down_weight[0], preferred_element_type=jnp.float32)
    home_out = home_out.astype(jnp.bfloat16).astype(jnp.float32)
    spare_out = jnp.dot(spare_hidden, spare_down[0], preferred_element_type=jnp.float32)
    home_at, home_scale = per_token(home_kept, home_flat, gate_weight, group_tokens, top_count)
    spare_at, spare_scale = per_token(spare_kept, spare_flat, gate_weight, group_tokens, top_count)
    partial = home_scale[:, None] * jnp.take(home_out, home_at, axis=0) + spare_scale[
        :, None
    ] * jnp.take(spare_out, spare_at, axis=0)
    mixed = lax.psum_scatter(partial, "ep", scatter_dimension=0, tiled=True)
    return mixed.astype(jnp.bfloat16)


def solution(mesh):
    return jax.shard_map(
        per_device,
        mesh=mesh,
        in_specs=(
            P("ep", "dp"),
            P("ep", None),
            P("ep", None),
            P(),
            P(),
            P("ep", None, None, "dp"),
            P("ep", None, "dp"),
            P("ep", None, None, "dp"),
            P("ep", None, "dp"),
        ),
        out_specs=P("ep", "dp"),
        check_vma=False,
    )
```

profile of v0, /device:TPU:0, one launch (start us, length us, event | category | flops | bytes accessed | tf_op | source)
XLA Modules:
  0.0 299.5 jit_solution(7959396471671987635)
XLA Ops:
  6.5 12.0 %all_gather.20 = bf16[64,4096]{1,0:T(8,128)(2,1)} all-gather(bf16[64,2048]{1,0:T(8,128)(2,1)} %param.13), channel_id=1, replica_groups=mesh['ep'=16,'dp'=2] {'dp'}, dimensions={1}, use_global_device_ids=true | all-gather | bytes 786432 | tf_op jit(solution)/shard_map/all_gather | solution.py:61
  18.6 1.2 dynamic_slice.6
  19.9 1.3 dynamic_slice.7
  21.2 22.4 %all-gather = s32[16,64,8]{1,2,0:T(8,128)S(1)} all-gather(s32[1,64,8]{1,2,0:T(8,128)} %bitcast.64), channel_id=1, replica_groups=mesh['ep'=16,'dp'=2] {'ep'}, dimensions={0}, use_global_device_ids=true | all-gather | bytes 34816 | tf_op jit(solution)/shard_map/all_gather | solution.py:63
  43.5 0.7 broadcast_compare_fusion
  44.8 0.9 compare_and_fusion
  45.7 0.4 reshape.117
  46.1 1.3 fusion.37
  48.1 1.3 compare_reduce_fusion
  50.0 0.3 compare_and_fusion.1
  50.3 0.4 reshape.114
  50.8 0.6 select_reduce_fusion.1
  51.6 18.5 %all-gather.1 = f32[16,64,8]{1,2,0:T(8,128)S(1)} all-gather(f32[1,64,8]{1,2,0:T(8,128)} %bitcast.65), channel_id=1, replica_groups=mesh['ep'=16,'dp'=2] {'ep'}, dimensions={0}, use_global_device_ids=true | all-gather | bytes 34816 | tf_op jit(solution)/shard_map/all_gather | solution.py:64
  70.2 1.1 copy.33
  71.4 0.3 reshape.116
  71.7 0.3 reshape.119
  72.3 0.2 select_reduce_fusion.2
  72.5 1.5 select_reduce_fusion.5
  74.1 20.5 %all-gather.5.cloned.1.call-done = bf16[1024,4096]{1,0:T(8,128)(2,1)} async-done(((bf16[64,4096]{1,0:T(8,128)(2,1)}), bf16[1024,4096]{1,0:T(8,128)(2,1)}) %all-gather.5.cloned.1.call-update) | async-done | bytes 8388624 | tf_op jit(solution)/shard_map/all_gather | solution.py:62
  94.6 13.0 %gather_fusion = bf16[512,4096]{1,0:T(8,128)(2,1)} fusion(bf16[1024,4096]{1,0:T(8,128)(2,1)} %all-gather.5.cloned.1.call-done, s32[1024]{0:T(1024)S(1)} %pad_clamp_fusion.1), kind=kCustom, calls=%fused_computation.clone | custom fusion | bytes 8390656 | tf_op jit(solution)/shard_map/jit(_take)/gather | solution.py:79
  107.7 8.3 %fusion = f32[512,2,512]{2,0,1:T(8,128)S(1)} fusion(bf16[4096,2,512]{2,1,0:T(2,128)(2,1)} %bitcast.66, bf16[512,4096]{1,0:T(8,128)(2,1)} %gather_fusion, pred[512]{0:T(512)(128)(4,1)S(1)} %compare_and_fusion.5), kind=kOutput, calls=%fused_computation.4 | convolution fusion | flops 4297064448 | bytes 14680576 | tf_op jit(solution)/shard_map/rd,djf->rjf/dot_general | solution.py:8
  116.0 1.1 fusion.25
  117.3 13.0 %gather_fusion.2 = bf16[512,4096]{1,0:T(8,128)(2,1)} fusion(bf16[1024,4096]{1,0:T(8,128)(2,1)} %all-gather.5.cloned.1.call-done, s32[1024]{0:T(1024)S(1)} %pad_clamp_fusion), kind=kCustom, calls=%fused_computation.2.clone | custom fusion | bytes 8390656 | tf_op jit(solution)/shard_map/jit(_take)/gather | solution.py:80
  130.4 5.8 %fusion.3 = f32[512,2,256]{2,0,1:T(8,128)S(1)} fusion(bf16[4096,2,256]{2,1,0:T(2,128)(2,1)} %bitcast.67, bf16[512,4096]{1,0:T(8,128)(2,1)} %gather_fusion.2, pred[512]{0:T(512)(128)(4,1)S(1)} %compare_and_fusion.4), kind=kOutput, calls=%fused_computation.9 | convolution fusion | flops 2149580800 | bytes 9437696 | tf_op jit(solution)/shard_map/rd,djf->rjf/dot_general | solution.py:8
  136.4 9.4 %all_gather.23 = bf16[512,512]{1,0:T(8,128)(2,1)S(1)} all-gather(bf16[512,256]{1,0:T(8,128)(2,1)S(1)} %fusion.29), channel_id=1, replica_groups=mesh['ep'=16,'dp'=2] {'dp'}, dimensions={1}, use_global_device_ids=true | all-gather | bytes 786432 | tf_op jit(solution)/shard_map/all_gather | solution.py:84
  145.7 3.3 %fusion.19 = f32[512,2048]{1,0:T(8,128)} fusion(bf16[512,512]{1,0:T(8,128)(2,1)S(1)} %all_gather.23, bf16[1,512,2048]{2,1,0:T(8,128)(2,1)S(1)} %copy-done), kind=kOutput, calls=%fused_computation.21 | convolution fusion | flops 1073741824 | bytes 6815744 | tf_op jit(solution)/shard_map/dot_general | solution.py:87
  149.0 11.2 %gather_fusion.3 = f32[1024,2048]{1,0:T(8,128)} fusion(f32[512,2048]{1,0:T(8,128)} %fusion.19, s32[1024]{0:T(1024)S(1)} %fusion.33), kind=kCustom, calls=%fused_computation.3.clone | custom fusion | bytes 16781312 | tf_op jit(solution)/shard_map/jit(_take)/gather | solution.py:92
  160.2 6.8 %fusion.16 = f32[512,2048]{1,0:T(8,128)} fusion(bf16[512,1024]{1,0:T(8,128)(2,1)} %all-gather.7.cloned.1.call-done, bf16[1,1024,2048]{2,1,0:T(8,128)(2,1)} %param.19), kind=kOutput, calls=%fused_computation.20 | convolution fusion | flops 2149580800 | bytes 9437184 | tf_op jit(solution)/shard_map/dot_general | solution.py:85
  167.0 11.3 %gather_fusion.1 = f32[1024,2048]{1,0:T(8,128)} fusion(f32[512,2048]{1,0:T(8,128)} %fusion.16, s32[1024]{0:T(1024)S(1)} %fusion.32), kind=kCustom, calls=%fused_computation.1.clone | custom fusion | bytes 16781312 | tf_op jit(solution)/shard_map/jit(_take)/gather | solution.py:90
  178.2 9.9 %fusion.2 = f32[1024,2048]{1,0:T(8,128)} fusion(f32[1024,2048]{1,0:T(8,128)} %gather_fusion.3, f32[1024,2048]{1,0:T(8,128)} %gather_fusion.1, f32[1024]{0:T(1024)S(1)} %get-tuple-element.8, f32[1024]{0:T(1024)S(1)} %get-tuple-element.6, pred[1024]{0:T(1024)(128)(4,1)S(1)} %get-tuple-element.19, pred[1024]{0:T(1024)(128)(4,1)S(1)} %get-tuple-element.20), kind=kLoop, calls=%fused_computation.7 | loop fusion | flops 10485760 | bytes 25176064 | tf_op jit(solution)/shard_map/add | solution.py:90
  188.2 103.1 %reduce-scatter.2.cloned.1.call-done = f32[64,2048]{1,0:T(8,128)} async-done(((f32[1024,2048]{1,0:T(8,128)}), f32[64,2048]{1,0:T(8,128)}) %reduce-scatter.2.cloned.1.call-update) | async-done | bytes 524304 | tf_op jit(solution)/shard_map/reduce_scatter | solution.py:93
  291.2 1.8 convert_element_type.31
  (37 shorter events, 1.8 us)
Async XLA Ops:
  6.5 139.2 %copy-start = (bf16[1,512,2048]{2,1,0:T(8,128)(2,1)S(1)}, bf16[1,512,2048]{2,1,0:T(8,128)(2,1)}, u32[]{:S(2)}) copy-start(bf16[1,512,2048]{2,1,0:T(8,128)(2,1)} %param.21) | copy-start | bytes 6291460
  6.5 88.1 %all-gather.5.cloned.1.call-start = ((), (), s32[]{:S(2)}) async-start(), calls=%async_computation.1 | async-start | bytes 8912896 | tf_op jit(solution)/shard_map/all_gather | solution.py:62
  18.6 141.6 %all-gather.7.cloned.1.call-start = ((), (), s32[]{:S(2)}) async-start(), calls=%async_computation.2 | async-start | bytes 1572864 | tf_op jit(solution)/shard_map/all_gather | solution.py:83
  117.1 174.1 %reduce-scatter.2.cloned.1.call-start = ((), (), s32[]{:S(2)}) async-start(), calls=%async_computation.3 | async-start | bytes 8912896 | tf_op jit(solution)/shard_map/reduce_scatter | solution.py:93
  188.1 104.9 %copy-start.1 = (bf16[1,512,2048]{2,1,0:T(8,128)(2,1)S(1)}, bf16[1,512,2048]{2,1,0:T(8,128)(2,1)}, u32[]{:S(2)}) copy-start(bf16[1,512,2048]{2,1,0:T(8,128)(2,1)} %param.21) | copy-start | bytes 6291460
Sparse Core Ops, SparseCore 0:
  18.7 75.8 all-gather.4
  117.2 19.5 all-gather.6
  188.3 102.8 reduce-scatter.1
where the time goes:
time: 300 us
  waiting for transfers between devices  124 us (41%)
  blocking collectives  62.2 us (21%)
  local copies, waits for them, and re-layouts  54.2 us (18%)
  matrix products  25.4 us (8%)
  other arithmetic  19.1 us (6%)
  between operations  14.6 us (5%)
    reduce_scatter x1, waiting for transfers between devices, per_device(): mixed = lax.psum_scatter(partial, 'ep', scatter_dimension=0, tiled=True)  103 us
    all_gather x1, blocking collectives, per_device(): every_id = lax.all_gather(expert_ids, 'ep', axis=0, tiled=True)  22.4 us
    all_gather x1, waiting for transfers between devices, per_device(): every_row = lax.all_gather(whole_rows, 'ep', axis=0, tiled=True)  20.5 us
    all_gather x1, blocking collectives, per_device(): every_logit = lax.all_gather(gate_logits, 'ep', axis=0, tiled=True)  18.5 us
    dot_general x2, matrix products, gate_up(): jnp.einsum('rd,djf->rjf', row_block, weight, preferred_element_type=jnp.f...  14.2 us
    gather x1, local copies, waits for them, and re-layouts, per_device(): spare_rows = jnp.take(every_row, spare_rows_of, axis=0)  13 us
    gather x1, local copies, waits for them, and re-layouts, per_device(): home_rows = jnp.take(every_row, home_rows_of, axis=0)  13 us
    all_gather x1, blocking collectives, per_device(): whole_rows = lax.all_gather(tokens, 'dp', axis=1, tiled=True)  12 us
  transfers between devices with their start and end apart: 3, of which 2 were waited for; matrix products, arithmetic and copies ran while one was open for 16% of the time, Pallas kernels for 0%

commit v1 on v0

--- a/solution.py
+++ b/solution.py
@@ -2,6 +2,25 @@
 import jax.numpy as jnp
 from jax import lax
 from jax.sharding import PartitionSpec as P
+
+
+def _save_tracks(q_in):
+    so_far_all = []
+    amount_of = lax.axis_size("ep")
+    for k in range(amount_of):
+        so_far_all.append((k, (k + 1) % amount_of))
+
+    def solve_task(left_arr):
+        if len(left_arr) == amount_of:
+            return left_arr
+        tile_out = solve_task(
+            [lax.ppermute(left_arr[0], axis_name="ep", perm=so_far_all), *left_arr]
+        )
+        return tile_out
+
+    v_next = jnp.concatenate(solve_task([q_in]), axis=0)
+    fresh = jnp.roll(v_next, (lax.axis_index("ep") + 1) * q_in.shape[0], 0)
+    return fresh
 
 
 def gate_up(row_block, weight):
@@ -59,7 +78,7 @@
     capacity = group_tokens * top_count // ep_count
     per_group = group_tokens * top_count
     whole_rows = lax.all_gather(tokens, "dp", axis=1, tiled=True)
-    every_row = lax.all_gather(whole_rows, "ep", axis=0, tiled=True)
+    every_row = _save_tracks(whole_rows)
     every_id = lax.all_gather(expert_ids, "ep", axis=0, tiled=True)
     every_logit = lax.all_gather(gate_logits, "ep", axis=0, tiled=True)
     ids = every_id.reshape(ep_count, per_group)

time: 300 us -> 470 us (1.57)
  waiting for transfers between devices: 124 us -> 240 us
  local copies, waits for them, and re-layouts: 54.2 us -> 111 us
  blocking collectives: 62.2 us -> 55.8 us
    ppermute x0 -> x15, waiting for transfers between devices: none -> 138 us  [solve_task(): lax.ppermute(left_arr[0], axis_name='ep', perm=so_far_all)]
    unnamed x4 -> x67, local copies, waits for them, and re-layouts: 0.01 us -> 47.5 us
    all_gather x1 -> x0, waiting for transfers between devices: 20.5 us -> none  [per_device(): every_row = lax.all_gather(whole_rows, 'ep', axis=0, tiled=True)]
    dynamic_slice x0 -> x1, local copies, waits for them, and re-layouts: none -> 7.73 us  [_save_tracks(): fresh = jnp.roll(v_next, (lax.axis_index('ep') + 1) * q_in.shape[0], 0)]
  transfers between devices with their start and end apart: 3 -> 17, of which waited for: 2 -> 14; matrix products, arithmetic and copies ran while one was open for 16% -> 10% of each run, Pallas kernels for 0% -> 0%
where the time goes in v1:
time: 470 us; the launch traced here: 469 us
  waiting for transfers between devices  240 us (51%)
  local copies, waits for them, and re-layouts  111 us (24%)
  blocking collectives  55.8 us (12%)
  matrix products  25.4 us (5%)
  other arithmetic  20.5 us (4%)
  between operations  15 us (3%)
    ppermute x15, waiting for transfers between devices, solve_task(): lax.ppermute(left_arr[0], axis_name='ep', perm=so_far_all)  138 us
    reduce_scatter x1, waiting for transfers between devices, per_device(): mixed = lax.psum_scatter(partial, 'ep', scatter_dimension=0, tiled=True)  102 us
    unnamed x67, local copies, waits for them, and re-layouts  47.5 us
    all_gather x1, blocking collectives, per_device(): every_id = lax.all_gather(expert_ids, 'ep', axis=0, tiled=True)  19.7 us
    all_gather x1, blocking collectives, per_device(): every_logit = lax.all_gather(gate_logits, 'ep', axis=0, tiled=True)  18.4 us
    dot_general x2, matrix products, gate_up(): jnp.einsum('rd,djf->rjf', row_block, weight, preferred_element_type=jnp.f...  14.2 us
    gather x1, local copies, waits for them, and re-layouts, per_device(): spare_rows = jnp.take(every_row, spare_rows_of, axis=0)  13.1 us
    gather x1, local copies, waits for them, and re-layouts, per_device(): home_rows = jnp.take(every_row, home_rows_of, axis=0)  13 us
  transfers between devices with their start and end apart: 17, of which 14 were waited for; matrix products, arithmetic and copies ran while one was open for 10% of the time, Pallas kernels for 0%

profile of v1, /device:TPU:0, one launch (start us, length us, event | category | flops | bytes accessed | tf_op | source)
XLA Modules:
  0.0 468.8 jit_solution(8179244283210899003)
XLA Ops:
  6.5 10.3 %all_gather.17 = bf16[64,4096]{1,0:T(8,128)(2,1)S(1)} all-gather(bf16[64,2048]{1,0:T(8,128)(2,1)} %param.13), channel_id=1, replica_groups=mesh['ep'=16,'dp'=2] {'dp'}, dimensions={1}, use_global_device_ids=true | all-gather | bytes 786432 | tf_op jit(solution)/shard_map/all_gather | solution.py:80
  16.9 11.3 %collective-permute-done = bf16[64,4096]{1,0:T(8,128)(2,1)S(1)} collective-permute-done((bf16[64,4096]{1,0:T(8,128)(2,1)S(1)}, bf16[64,4096]{1,0:T(8,128)(2,1)S(1)}, u32[]{:S(2)}, u32[]{:S(2)}) %collective-permute-start) | collective-permute-done | bytes 524320 | tf_op jit(solution)/shard_map/ppermute | solution.py:17
  29.0 11.3 %collective-permute-done.1 = bf16[64,4096]{1,0:T(8,128)(2,1)S(1)} collective-permute-done((bf16[64,4096]{1,0:T(8,128)(2,1)S(1)}, bf16[64,4096]{1,0:T(8,128)(2,1)S(1)}, u32[]{:S(2)}, u32[]{:S(2)}) %collective-permute-start.1) | collective-permute-done | bytes 524320 | tf_op jit(solution)/shard_map/ppermute | solution.py:17
  41.1 11.3 %collective-permute-done.2 = bf16[64,4096]{1,0:T(8,128)(2,1)S(1)} collective-permute-done((bf16[64,4096]{1,0:T(8,128)(2,1)S(1)}, bf16[64,4096]{1,0:T(8,128)(2,1)S(1)}, u32[]{:S(2)}, u32[]{:S(2)}) %collective-permute-start.2) | collective-permute-done | bytes 524320 | tf_op jit(solution)/shard_map/ppermute | solution.py:17
  53.2 11.3 %collective-permute-done.3 = bf16[64,4096]{1,0:T(8,128)(2,1)S(1)} collective-permute-done((bf16[64,4096]{1,0:T(8,128)(2,1)S(1)}, bf16[64,4096]{1,0:T(8,128)(2,1)S(1)}, u32[]{:S(2)}, u32[]{:S(2)}) %collective-permute-start.3) | collective-permute-done | bytes 524320 | tf_op jit(solution)/shard_map/ppermute | solution.py:17
  65.3 11.3 %collective-permute-done.4 = bf16[64,4096]{1,0:T(8,128)(2,1)S(1)} collective-permute-done((bf16[64,4096]{1,0:T(8,128)(2,1)S(1)}, bf16[64,4096]{1,0:T(8,128)(2,1)S(1)}, u32[]{:S(2)}, u32[]{:S(2)}) %collective-permute-start.4) | collective-permute-done | bytes 524320 | tf_op jit(solution)/shard_map/ppermute | solution.py:17
  77.5 11.3 %collective-permute-done.5 = bf16[64,4096]{1,0:T(8,128)(2,1)S(1)} collective-permute-done((bf16[64,4096]{1,0:T(8,128)(2,1)S(1)}, bf16[64,4096]{1,0:T(8,128)(2,1)S(1)}, u32[]{:S(2)}, u32[]{:S(2)}) %collective-permute-start.5) | collective-permute-done | bytes 524320 | tf_op jit(solution)/shard_map/ppermute | solution.py:17
  89.6 11.3 %collective-permute-done.6 = bf16[64,4096]{1,0:T(8,128)(2,1)S(1)} collective-permute-done((bf16[64,4096]{1,0:T(8,128)(2,1)S(1)}, bf16[64,4096]{1,0:T(8,128)(2,1)S(1)}, u32[]{:S(2)}, u32[]{:S(2)}) %collective-permute-start.6) | collective-permute-done | bytes 524320 | tf_op jit(solution)/shard_map/ppermute | solution.py:17
  102.2 19.7 %all-gather = s32[16,64,8]{1,2,0:T(8,128)S(1)} all-gather(s32[1,64,8]{1,2,0:T(8,128)} %bitcast.64), channel_id=1, replica_groups=mesh['ep'=16,'dp'=2] {'ep'}, dimensions={0}, use_global_device_ids=true | all-gather | bytes 34816 | tf_op jit(solution)/shard_map/all_gather | solution.py:82
  128.7 4.8 %collective-permute-done.8 = bf16[64,4096]{1,0:T(8,128)(2,1)} collective-permute-done((bf16[64,4096]{1,0:T(8,128)(2,1)}, bf16[64,4096]{1,0:T(8,128)(2,1)}, u32[]{:S(2)}, u32[]{:S(2)}) %collective-permute-start.8) | collective-permute-done | bytes 524320 | tf_op jit(solution)/shard_map/ppermute | solution.py:17
  134.5 10.5 %collective-permute-done.9 = bf16[64,4096]{1,0:T(8,128)(2,1)S(1)} collective-permute-done((bf16[64,4096]{1,0:T(8,128)(2,1)}, bf16[64,4096]{1,0:T(8,128)(2,1)S(1)}, u32[]{:S(2)}, u32[]{:S(2)}) %collective-permute-start.9) | collective-permute-done | bytes 524320 | tf_op jit(solution)/shard_map/ppermute | solution.py:17
  146.2 11.0 %collective-permute-done.10 = bf16[64,4096]{1,0:T(8,128)(2,1)} collective-permute-done((bf16[64,4096]{1,0:T(8,128)(2,1)S(1)}, bf16[64,4096]{1,0:T(8,128)(2,1)}, u32[]{:S(2)}, u32[]{:S(2)}) %collective-permute-start.10) | collective-permute-done | bytes 524320 | tf_op jit(solution)/shard_map/ppermute | solution.py:17
  160.2 18.4 %all-gather.1 = f32[16,64,8]{1,2,0:T(8,128)S(1)} all-gather(f32[1,64,8]{1,2,0:T(8,128)} %bitcast.65), channel_id=1, replica_groups=mesh['ep'=16,'dp'=2] {'ep'}, dimensions={0}, use_global_device_ids=true | all-gather | bytes 34816 | tf_op jit(solution)/shard_map/all_gather | solution.py:83
  183.1 10.1 %collective-permute-done.12 = bf16[64,4096]{1,0:T(8,128)(2,1)S(1)} collective-permute-done((bf16[64,4096]{1,0:T(8,128)(2,1)}, bf16[64,4096]{1,0:T(8,128)(2,1)S(1)}, u32[]{:S(2)}, u32[]{:S(2)}) %collective-permute-start.12) | collective-permute-done | bytes 524320 | tf_op jit(solution)/shard_map/ppermute | solution.py:17
  193.4 11.0 %collective-permute-done.13 = bf16[64,4096]{1,0:T(8,128)(2,1)S(1)} collective-permute-done((bf16[64,4096]{1,0:T(8,128)(2,1)S(1)}, bf16[64,4096]{1,0:T(8,128)(2,1)S(1)}, u32[]{:S(2)}, u32[]{:S(2)}) %collective-permute-start.13) | collective-permute-done | bytes 524320 | tf_op jit(solution)/shard_map/ppermute | solution.py:17
  204.5 11.3 %collective-permute-done.14 = bf16[64,4096]{1,0:T(8,128)(2,1)S(1)} collective-permute-done((bf16[64,4096]{1,0:T(8,128)(2,1)S(1)}, bf16[64,4096]{1,0:T(8,128)(2,1)S(1)}, u32[]{:S(2)}, u32[]{:S(2)}) %collective-permute-start.14) | collective-permute-done | bytes 524320 | tf_op jit(solution)/shard_map/ppermute | solution.py:17
  218.3 1.9 constant_dynamic-update-slice_fusion.28
  231.5 1.9 constant_dynamic-update-slice_fusion.21
  233.4 1.9 constant_dynamic-update-slice_fusion.20
  243.3 1.9 constant_dynamic-update-slice_fusion.12
  258.5 7.7 %constant_dynamic-slice_fusion = bf16[1024,4096]{1,0:T(8,128)(2,1)} fusion(bf16[2048,4096]{1,0:T(8,128)(2,1)} %constant_dynamic-update-slice_fusion, s32[]{:T(128)S(6)} %select_n.81), kind=kLoop, calls=%fused_computation.114 | loop fusion | bytes 16777220 | tf_op jit(solution)/shard_map/jit(_roll_dynamic)/dynamic_slice | solution.py:22
  266.2 13.0 %gather_fusion = bf16[512,4096]{1,0:T(8,128)(2,1)} fusion(bf16[1024,4096]{1,0:T(8,128)(2,1)} %constant_dynamic-slice_fusion, s32[1024]{0:T(1024)S(1)} %get-tuple-element.20), kind=kCustom, calls=%fused_computation.clone | custom fusion | bytes 8390656 | tf_op jit(solution)/shard_map/jit(_take)/gather | solution.py:98
  279.2 8.3 %fusion = f32[512,2,512]{2,0,1:T(8,128)S(1)} fusion(bf16[4096,2,512]{2,1,0:T(2,128)(2,1)} %bitcast.66, bf16[512,4096]{1,0:T(8,128)(2,1)} %gather_fusion, pred[512]{0:T(512)(128)(4,1)S(1)} %compare_and_fusion.5), kind=kOutput, calls=%fused_computation.4 | convolution fusion | flops 4297064448 | bytes 14680576 | tf_op jit(solution)/shard_map/rd,djf->rjf/dot_general | solution.py:27
  289.0 13.1 %gather_fusion.2 = bf16[512,4096]{1,0:T(8,128)(2,1)} fusion(bf16[1024,4096]{1,0:T(8,128)(2,1)} %constant_dynamic-slice_fusion, s32[1024]{0:T(1024)S(1)} %get-tuple-element.19), kind=kCustom, calls=%fused_computation.2.clone | custom fusion | bytes 8390656 | tf_op jit(solution)/shard_map/jit(_take)/gather | solution.py:99
  302.1 5.8 %fusion.3 = f32[512,2,256]{2,0,1:T(8,128)S(1)} fusion(bf16[4096,2,256]{2,1,0:T(2,128)(2,1)} %bitcast.67, bf16[512,4096]{1,0:T(8,128)(2,1)} %gather_fusion.2, pred[512]{0:T(512)(128)(4,1)S(1)} %compare_and_fusion.4), kind=kOutput, calls=%fused_computation.9 | convolution fusion | flops 2149580800 | bytes 9437696 | tf_op jit(solution)/shard_map/rd,djf->rjf/dot_general | solution.py:27
  308.1 7.3 %all_gather.19 = bf16[512,512]{1,0:T(8,128)(2,1)S(1)} all-gather(bf16[512,256]{1,0:T(8,128)(2,1)S(1)} %fusion.29), channel_id=1, replica_groups=mesh['ep'=16,'dp'=2] {'dp'}, dimensions={1}, use_global_device_ids=true | all-gather | bytes 786432 | tf_op jit(solution)/shard_map/all_gather | solution.py:103
  315.4 3.3 fusion.19
  318.7 11.2 %gather_fusion.3 = f32[1024,2048]{1,0:T(8,128)} fusion(f32[512,2048]{1,0:T(8,128)} %fusion.19, s32[1024]{0:T(1024)S(1)} %get-tuple-element.22), kind=kCustom, calls=%fused_computation.3.clone | custom fusion | bytes 16781312 | tf_op jit(solution)/shard_map/jit(_take)/gather | solution.py:111
  329.9 6.8 %fusion.16 = f32[512,2048]{1,0:T(8,128)} fusion(bf16[512,1024]{1,0:T(8,128)(2,1)} %all-gather.4.cloned.1.call-done, bf16[1,1024,2048]{2,1,0:T(8,128)(2,1)} %param.19), kind=kOutput, calls=%fused_computation.20 | convolution fusion | flops 2149580800 | bytes 9437184 | tf_op jit(solution)/shard_map/dot_general | solution.py:104
  336.7 11.2 %gather_fusion.1 = f32[1024,2048]{1,0:T(8,128)} fusion(f32[512,2048]{1,0:T(8,128)} %fusion.16, s32[1024]{0:T(1024)S(1)} %get-tuple-element.21), kind=kCustom, calls=%fused_computation.1.clone | custom fusion | bytes 16781312 | tf_op jit(solution)/shard_map/jit(_take)/gather | solution.py:109
  347.9 10.1 %fusion.2 = f32[1024,2048]{1,0:T(8,128)} fusion(f32[1024,2048]{1,0:T(8,128)} %gather_fusion.3, f32[1024,2048]{1,0:T(8,128)} %gather_fusion.1, f32[1024]{0:T(1024)S(1)} %get-tuple-element.8, f32[1024]{0:T(1024)S(1)} %get-tuple-element.6, pred[1024]{0:T(1024)(128)(4,1)S(1)} %get-tuple-element.23, pred[1024]{0:T(1024)(128)(4,1)S(1)} %get-tuple-element.24), kind=kLoop, calls=%fused_computation.7 | loop fusion | flops 10485760 | bytes 25176064 | tf_op jit(solution)/shard_map/add | solution.py:109
  358.0 102.2 %reduce-scatter.2.cloned.1.call-done = f32[64,2048]{1,0:T(8,128)} async-done(((f32[1024,2048]{1,0:T(8,128)}), f32[64,2048]{1,0:T(8,128)}) %reduce-scatter.2.cloned.1.call-update) | async-done | bytes 524304 | tf_op jit(solution)/shard_map/reduce_scatter | solution.py:112
  (127 shorter events, 59.8 us)
Async XLA Ops:
  6.5 308.9 %copy-start = (bf16[1,512,2048]{2,1,0:T(8,128)(2,1)S(1)}, bf16[1,512,2048]{2,1,0:T(8,128)(2,1)}, u32[]{:S(2)}) copy-start(bf16[1,512,2048]{2,1,0:T(8,128)(2,1)} %param.21) | copy-start | bytes 6291460
  6.5 323.4 %all-gather.4.cloned.1.call-start = ((), (), s32[]{:S(2)}) async-start(), calls=%async_computation.1 | async-start | bytes 1572864 | tf_op jit(solution)/shard_map/all_gather | solution.py:102
  16.9 11.3 %collective-permute-start = (bf16[64,4096]{1,0:T(8,128)(2,1)S(1)}, bf16[64,4096]{1,0:T(8,128)(2,1)S(1)}, u32[]{:S(2)}, u32[]{:S(2)}) collective-permute-start(bf16[64,4096]{1,0:T(8,128)(2,1)S(1)} %all_gather.17), channel_id=1, source_target_pairs={{0,2},{2,4},{4,6},{6,8},{8,10},{10,12},{12,14},{14,16},{16,18},{18... | collective-permute-start | bytes 1572872 | tf_op jit(solution)/shard_map/ppermute | solution.py:17
  28.2 0.8 copy-start.2
  29.0 11.3 %collective-permute-start.1 = (bf16[64,4096]{1,0:T(8,128)(2,1)S(1)}, bf16[64,4096]{1,0:T(8,128)(2,1)S(1)}, u32[]{:S(2)}, u32[]{:S(2)}) collective-permute-start(bf16[64,4096]{1,0:T(8,128)(2,1)S(1)} %collective-permute-done), channel_id=1, source_target_pairs={{0,2},{2,4},{4,6},{6,8},{8,10},{10,12},{12,14},{14,16},{16,18},{18... | collective-permute-start | bytes 1572872 | tf_op jit(solution)/shard_map/ppermute | solution.py:17
  40.3 0.8 copy-start.4
  41.1 11.3 %collective-permute-start.2 = (bf16[64,4096]{1,0:T(8,128)(2,1)S(1)}, bf16[64,4096]{1,0:T(8,128)(2,1)S(1)}, u32[]{:S(2)}, u32[]{:S(2)}) collective-permute-start(bf16[64,4096]{1,0:T(8,128)(2,1)S(1)} %collective-permute-done.1), channel_id=1, source_target_pairs={{0,2},{2,4},{4,6},{6,8},{8,10},{10,12},{12,14},{14,16},{16,18},{18... | collective-permute-start | bytes 1572872 | tf_op jit(solution)/shard_map/ppermute | solution.py:17
  53.2 11.3 %collective-permute-start.3 = (bf16[64,4096]{1,0:T(8,128)(2,1)S(1)}, bf16[64,4096]{1,0:T(8,128)(2,1)S(1)}, u32[]{:S(2)}, u32[]{:S(2)}) collective-permute-start(bf16[64,4096]{1,0:T(8,128)(2,1)S(1)} %collective-permute-done.2), channel_id=1, source_target_pairs={{0,2},{2,4},{4,6},{6,8},{8,10},{10,12},{12,14},{14,16},{16,18},{18... | collective-permute-start | bytes 1572872 | tf_op jit(solution)/shard_map/ppermute | solution.py:17
  64.5 0.8 copy-start.8
  65.3 11.3 %collective-permute-start.4 = (bf16[64,4096]{1,0:T(8,128)(2,1)S(1)}, bf16[64,4096]{1,0:T(8,128)(2,1)S(1)}, u32[]{:S(2)}, u32[]{:S(2)}) collective-permute-start(bf16[64,4096]{1,0:T(8,128)(2,1)S(1)} %collective-permute-done.3), channel_id=1, source_target_pairs={{0,2},{2,4},{4,6},{6,8},{8,10},{10,12},{12,14},{14,16},{16,18},{18... | collective-permute-start | bytes 1572872 | tf_op jit(solution)/shard_map/ppermute | solution.py:17
  77.5 11.3 %collective-permute-start.5 = (bf16[64,4096]{1,0:T(8,128)(2,1)S(1)}, bf16[64,4096]{1,0:T(8,128)(2,1)S(1)}, u32[]{:S(2)}, u32[]{:S(2)}) collective-permute-start(bf16[64,4096]{1,0:T(8,128)(2,1)S(1)} %collective-permute-done.4), channel_id=1, source_target_pairs={{0,2},{2,4},{4,6},{6,8},{8,10},{10,12},{12,14},{14,16},{16,18},{18... | collective-permute-start | bytes 1572872 | tf_op jit(solution)/shard_map/ppermute | solution.py:17
  88.8 0.8 copy-start.12
  89.6 11.3 %collective-permute-start.6 = (bf16[64,4096]{1,0:T(8,128)(2,1)S(1)}, bf16[64,4096]{1,0:T(8,128)(2,1)S(1)}, u32[]{:S(2)}, u32[]{:S(2)}) collective-permute-start(bf16[64,4096]{1,0:T(8,128)(2,1)S(1)} %collective-permute-done.5), channel_id=1, source_target_pairs={{0,2},{2,4},{4,6},{6,8},{8,10},{10,12},{12,14},{14,16},{16,18},{18... | collective-permute-start | bytes 1572872 | tf_op jit(solution)/shard_map/ppermute | solution.py:17
  100.9 59.0 %copy-start.14 = (bf16[64,4096]{1,0:T(8,128)(2,1)}, bf16[64,4096]{1,0:T(8,128)(2,1)S(1)}, u32[]{:S(2)}) copy-start(bf16[64,4096]{1,0:T(8,128)(2,1)S(1)} %collective-permute-done.6) | copy-start | bytes 1572868
  100.9 21.0 %collective-permute-start.7 = (bf16[64,4096]{1,0:T(8,128)(2,1)S(1)}, bf16[64,4096]{1,0:T(8,128)(2,1)}, u32[]{:S(2)}, u32[]{:S(2)}) collective-permute-start(bf16[64,4096]{1,0:T(8,128)(2,1)S(1)} %collective-permute-done.6), channel_id=1, source_target_pairs={{0,2},{2,4},{4,6},{6,8},{8,10},{10,12},{12,14},{14,16},{16,18},{18... | collective-permute-start | bytes 1572872 | tf_op jit(solution)/shard_map/ppermute | solution.py:17
  121.9 11.6 %collective-permute-start.8 = (bf16[64,4096]{1,0:T(8,128)(2,1)}, bf16[64,4096]{1,0:T(8,128)(2,1)}, u32[]{:S(2)}, u32[]{:S(2)}) collective-permute-start(bf16[64,4096]{1,0:T(8,128)(2,1)} %collective-permute-done.7), channel_id=1, source_target_pairs={{0,2},{2,4},{4,6},{6,8},{8,10},{10,12},{12,14},{14,16},{16,18},{18... | collective-permute-start | bytes 1572872 | tf_op jit(solution)/shard_map/ppermute | solution.py:17
  133.5 11.5 %collective-permute-start.9 = (bf16[64,4096]{1,0:T(8,128)(2,1)}, bf16[64,4096]{1,0:T(8,128)(2,1)S(1)}, u32[]{:S(2)}, u32[]{:S(2)}) collective-permute-start(bf16[64,4096]{1,0:T(8,128)(2,1)} %collective-permute-done.8), channel_id=1, source_target_pairs={{0,2},{2,4},{4,6},{6,8},{8,10},{10,12},{12,14},{14,16},{16,18},{18... | collective-permute-start | bytes 1572872 | tf_op jit(solution)/shard_map/ppermute | solution.py:17
  145.8 11.4 %collective-permute-start.10 = (bf16[64,4096]{1,0:T(8,128)(2,1)S(1)}, bf16[64,4096]{1,0:T(8,128)(2,1)}, u32[]{:S(2)}, u32[]{:S(2)}) collective-permute-start(bf16[64,4096]{1,0:T(8,128)(2,1)S(1)} %collective-permute-done.9), channel_id=1, source_target_pairs={{0,2},{2,4},{4,6},{6,8},{8,10},{10,12},{12,14},{14,16},{16,18},{18... | collective-permute-start | bytes 1572872 | tf_op jit(solution)/shard_map/ppermute | solution.py:17
  157.3 24.3 %collective-permute-start.11 = (bf16[64,4096]{1,0:T(8,128)(2,1)}, bf16[64,4096]{1,0:T(8,128)(2,1)}, u32[]{:S(2)}, u32[]{:S(2)}) collective-permute-start(bf16[64,4096]{1,0:T(8,128)(2,1)} %collective-permute-done.10), channel_id=1, source_target_pairs={{0,2},{2,4},{4,6},{6,8},{8,10},{10,12},{12,14},{14,16},{16,18},{18... | collective-permute-start | bytes 1572872 | tf_op jit(solution)/shard_map/ppermute | solution.py:17
  179.8 59.2 %copy-start.3 = (bf16[64,4096]{1,0:T(8,128)(2,1)S(1)}, bf16[64,4096]{1,0:T(8,128)(2,1)}, u32[]{:S(2)}) copy-start(bf16[64,4096]{1,0:T(8,128)(2,1)} %copy-done.2) | copy-start | bytes 1572868
  179.8 67.2 %copy-start.17 = (bf16[64,4096]{1,0:T(8,128)(2,1)S(1)}, bf16[64,4096]{1,0:T(8,128)(2,1)}, u32[]{:S(2)}) copy-start(bf16[64,4096]{1,0:T(8,128)(2,1)} %copy-done.16) | copy-start | bytes 1572868
  179.8 71.8 %copy-start.15 = (bf16[64,4096]{1,0:T(8,128)(2,1)S(1)}, bf16[64,4096]{1,0:T(8,128)(2,1)}, u32[]{:S(2)}) copy-start(bf16[64,4096]{1,0:T(8,128)(2,1)} %copy-done.14) | copy-start | bytes 1572868
  179.9 72.6 %copy-start.13 = (bf16[64,4096]{1,0:T(8,128)(2,1)S(1)}, bf16[64,4096]{1,0:T(8,128)(2,1)}, u32[]{:S(2)}) copy-start(bf16[64,4096]{1,0:T(8,128)(2,1)} %copy-done.12) | copy-start | bytes 1572868
  179.9 73.5 %copy-start.11 = (bf16[64,4096]{1,0:T(8,128)(2,1)S(1)}, bf16[64,4096]{1,0:T(8,128)(2,1)}, u32[]{:S(2)}) copy-start(bf16[64,4096]{1,0:T(8,128)(2,1)} %copy-done.10) | copy-start | bytes 1572868
  179.9 74.3 %copy-start.9 = (bf16[64,4096]{1,0:T(8,128)(2,1)S(1)}, bf16[64,4096]{1,0:T(8,128)(2,1)}, u32[]{:S(2)}) copy-start(bf16[64,4096]{1,0:T(8,128)(2,1)} %copy-done.8) | copy-start | bytes 1572868
  179.9 75.2 %copy-start.7 = (bf16[64,4096]{1,0:T(8,128)(2,1)S(1)}, bf16[64,4096]{1,0:T(8,128)(2,1)}, u32[]{:S(2)}) copy-start(bf16[64,4096]{1,0:T(8,128)(2,1)} %copy-done.6) | copy-start | bytes 1572868
  179.9 76.0 %copy-start.5 = (bf16[64,4096]{1,0:T(8,128)(2,1)S(1)}, bf16[64,4096]{1,0:T(8,128)(2,1)}, u32[]{:S(2)}) copy-start(bf16[64,4096]{1,0:T(8,128)(2,1)} %copy-done.4) | copy-start | bytes 1572868
  181.6 11.6 %collective-permute-start.12 = (bf16[64,4096]{1,0:T(8,128)(2,1)}, bf16[64,4096]{1,0:T(8,128)(2,1)S(1)}, u32[]{:S(2)}, u32[]{:S(2)}) collective-permute-start(bf16[64,4096]{1,0:T(8,128)(2,1)} %collective-permute-done.11), channel_id=1, source_target_pairs={{0,2},{2,4},{4,6},{6,8},{8,10},{10,12},{12,14},{14,16},{16,18},{18... | collective-permute-start | bytes 1572872 | tf_op jit(solution)/shard_map/ppermute | solution.py:17
  193.2 11.3 %collective-permute-start.13 = (bf16[64,4096]{1,0:T(8,128)(2,1)S(1)}, bf16[64,4096]{1,0:T(8,128)(2,1)S(1)}, u32[]{:S(2)}, u32[]{:S(2)}) collective-permute-start(bf16[64,4096]{1,0:T(8,128)(2,1)S(1)} %collective-permute-done.12), channel_id=1, source_target_pairs={{0,2},{2,4},{4,6},{6,8},{8,10},{10,12},{12,14},{14,16},{16,18},{18... | collective-permute-start | bytes 1572872 | tf_op jit(solution)/shard_map/ppermute | solution.py:17
  204.5 11.3 %collective-permute-start.14 = (bf16[64,4096]{1,0:T(8,128)(2,1)S(1)}, bf16[64,4096]{1,0:T(8,128)(2,1)S(1)}, u32[]{:S(2)}, u32[]{:S(2)}) collective-permute-start(bf16[64,4096]{1,0:T(8,128)(2,1)S(1)} %collective-permute-done.13), channel_id=1, source_target_pairs={{0,2},{2,4},{4,6},{6,8},{8,10},{10,12},{12,14},{14,16},{16,18},{18... | collective-permute-start | bytes 1572872 | tf_op jit(solution)/shard_map/ppermute | solution.py:17
  288.7 171.4 %reduce-scatter.2.cloned.1.call-start = ((), (), s32[]{:S(2)}) async-start(), calls=%async_computation.2 | async-start | bytes 8912896 | tf_op jit(solution)/shard_map/reduce_scatter | solution.py:112
  347.9 114.1 %copy-start.1 = (bf16[1,512,2048]{2,1,0:T(8,128)(2,1)S(1)}, bf16[1,512,2048]{2,1,0:T(8,128)(2,1)}, u32[]{:S(2)}) copy-start(bf16[1,512,2048]{2,1,0:T(8,128)(2,1)} %param.21) | copy-start | bytes 6291460
  (3 other events, 2.4 us)
Sparse Core Ops, SparseCore 0:
  288.9 21.1 all-gather.3
  358.1 102.0 reduce-scatter.1
